TPU v7x, 256 devices: a whole 4x4x8 slice. The times are simulated.
256 devices in a mesh: walker: 32 (over z, x_lo, core), vec: 8 (over x_hi, y).
Axes of the slice: x: 4 (x_hi: 2, x_lo: 2; x = x_hi * 2 + x_lo), y: 4, z: 8, core: 2. Of those that a mesh axis runs over, the one named last changes fastest.
Arguments:
- copy_counts: int32 [32], P('walker'), may hold values from 0 to 2, as said below
- panels: bfloat16 [32, 200, 2048], P('walker', 'vec'), may hold values from -6 to 6
- inverse_intersection: bfloat16 [32, 200, 200], P('walker', 'vec'), may hold values from -0.4375 to 0.4375
- trial_orbitals: bfloat16 [200, 2048], replicated, may hold values from -0.0625 to 0.0625
- chol_tiles: bfloat16 [256, 128, 128], P(('walker', 'vec')), may hold values from -1.25 to 1.25
- tile_blocks: int32 [256, 2], replicated, may hold values from 0 to 15
- aux_fields: float32 [32, 64], P('walker'), may hold values from -6 to 6
Outputs:
- new_panels: bfloat16 [32, 200, 2048], P('walker', 'vec')
Inputs may be any that keep to these rules, and one draw needn't show every extreme that they name: `copy_counts`: for k = 0 .. 32 let e_k be the sum of the counts of walkers 0 .. k - 1 minus k. Every e_k lies in 0 .. 1, the first and the last are 0 (the counts sum to 32), and e_k = 1 for at least one k. Some walker has exactly 2 copies.
All inputs are finite; a program needn't handle non-finite values.
Results may differ from a plain program's by a relative error of at most 0.007.
Values may be sent and summed in bfloat16 or wider, within the bound.
No kernel may reach another device: no remote copies, remote signals or barrier semaphores. Data moves between devices by JAX's collectives and lax.ppermute only.
A program may use at most 64 MiB of HBM per device.

v0:
```python
import math
import jax
import jax.numpy as jnp
from jax import lax
from jax.sharding import PartitionSpec as P

KT = 4
TERMS = 3
TIME_STEP_ROOT = 0.1


def from_behind(value, axis, steps):
    count = lax.axis_size(axis)
    leading, last = (max(0, -steps), min(count, count - steps))
    return lax.ppermute(value, axis, [(source, source + steps) for source in range(leading, last)])


def tile_bias(tile_piece, row_blocks, col_blocks, panel_blocks, green_blocks):
    chosen = jnp.take(green_blocks, col_blocks, axis=2)
    product = jnp.einsum("wirl,rkl->wirk", chosen, tile_piece, preferred_element_type=jnp.float32)
    facing = jnp.take(panel_blocks, row_blocks, axis=2)
    return jnp.sum(product * facing, axis=(1, 3))


def force_bias(walker_panels, walker_inverse, trial_orbitals, chol_tiles, tile_blocks):
    walkers, cols_local, orbitals = walker_panels.shape
    tile_size = chol_tiles.shape[1]
    block_count = orbitals // tile_size
    tiles_total = tile_blocks.shape[0]
    green_rows = jnp.einsum(
        "wij,jm->wim", walker_inverse, trial_orbitals, preferred_element_type=jnp.float32
    ).astype(jnp.bfloat16)
    panel_blocks = walker_panels.reshape(walkers, cols_local, block_count, tile_size)
    green_blocks = green_rows.reshape(walkers, cols_local, block_count, tile_size)
    tile_piece = lax.all_gather(chol_tiles, ("walker", "vec"), axis=0, tiled=True)
    contrib = tile_bias(
        tile_piece, tile_blocks[:, 0], tile_blocks[:, 1], panel_blocks, green_blocks
    )
    partial_bias = contrib
    stored = tile_piece
    partial_bias, stored = (partial_bias, stored)
    per_vector = partial_bias.reshape(walkers, tiles_total // KT, KT).sum(axis=2)
    summed_bias = lax.psum(per_vector, "vec")
    return (jnp.clip(TIME_STEP_ROOT * summed_bias, -1.0, 1.0), stored)


def propagate(start_panels, scales, stored, tile_blocks):
    slot_count, cols_local, orbitals = start_panels.shape
    tile_size = stored.shape[1]
    block_count = orbitals // tile_size
    tiles_total = stored.shape[0]
    step_tiles = math.gcd(tiles_total, 256)
    rows_hot = (
        tile_blocks[:, 0][None, :] == jnp.arange(block_count, dtype=jnp.int32)[:, None]
    ).astype(jnp.float32)
    weights = jnp.repeat(scales, KT, axis=1)[:, None, :] * rows_hot[None, :, :]
    col_blocks = tile_blocks[:, 1]
    running = start_panels.astype(jnp.float32)
    series = start_panels
    for degree in range(1, TERMS + 1):
        series_blocks = series.reshape(slot_count, cols_local, block_count, tile_size)

        def add_block(block_index, summed):
            chosen = jnp.take(series_blocks, col_blocks, axis=2)
            product = jnp.einsum(
                "qitl,tkl->qitk", chosen, stored, preferred_element_type=jnp.float32
            )
            return summed + jnp.einsum(
                "qitk,qat->qiak", product, weights, precision=lax.Precision.HIGHEST
            )

        result = lax.fori_loop(
            0,
            tiles_total // step_tiles,
            add_block,
            jnp.zeros((slot_count, cols_local, block_count, tile_size), jnp.float32),
        )
        series = (result / degree).reshape(slot_count, cols_local, orbitals).astype(jnp.bfloat16)
        running = running + series.astype(jnp.float32)
    return running.astype(jnp.bfloat16)


def shards(
    copy_counts, panels, inverse_intersection, trial_orbitals, chol_tiles, tile_blocks, aux_fields
):
    walkers = panels.shape[0]
    every_count = lax.all_gather(copy_counts, "walker", axis=0, tiled=True)
    running_sum = jnp.cumsum(every_count)
    first_slot = lax.axis_index("walker") * walkers
    bias, stored = force_bias(panels, inverse_intersection, trial_orbitals, chol_tiles, tile_blocks)
    own_sums = lax.dynamic_slice_in_dim(running_sum, first_slot, walkers, 0)
    surplus = own_sums[0] - copy_counts[0] - first_slot
    new_index = first_slot + jnp.arange(2 * walkers, dtype=jnp.int32)
    parent = jnp.minimum(
        jnp.sum((own_sums[None, :] <= new_index[:, None]).astype(jnp.int32), axis=1), walkers - 1
    )
    right_fields = from_behind(aux_fields, "walker", -1)
    field_pool = jnp.concatenate([aux_fields, right_fields], axis=0)
    scales = TIME_STEP_ROOT * (field_pool - jnp.take(bias, parent, axis=0))
    copies = propagate(jnp.take(panels, parent, axis=0), scales, stored, tile_blocks)
    arrived = from_behind(copies[walkers:], "walker", 1)
    keep_own = (jnp.arange(walkers, dtype=jnp.int32) >= surplus)[:, None, None]
    return jnp.where(keep_own, copies[:walkers], arrived)


def solution(mesh):
    return jax.shard_map(
        shards,
        mesh=mesh,
        in_specs=(
            P("walker"),
            P("walker", "vec", None),
            P("walker", "vec", None),
            P(),
            P(("walker", "vec"), None, None),
            P(),
            P("walker", None),
        ),
        out_specs=P("walker", "vec", None),
        check_vma=False,
    )
```

profile of v0, /device:TPU:104, one launch (start us, length us, event | category | flops | bytes accessed | tf_op | source)
XLA Modules:
  0.0 873.2 jit_solution(1294676800339931212)
XLA Ops:
  6.5 0.0 copy-start
  6.5 0.0 copy-start.3
  6.5 0.0 all-gather.2.cloned.1.call-start
  6.5 0.7 all-gather.2.cloned.1.call-update
  7.3 2.4 collective-permute-start
  9.7 0.0 copy-done
  9.7 1.0 convolution_convert_fusion
  10.8 0.9 copy.50
  12.4 1.2 dynamic-slice.1
  13.6 0.7 dynamic-update-slice
  14.3 16.2 %all-reduce = s32[32]{0:T(128)S(1)} all-reduce(s32[32]{0:T(128)S(1)} %dynamic-update-slice), channel_id=1, replica_groups=mesh['walker'=32,'vec'=8] {'walker'}, use_global_device_ids=true, to_apply=%add | all-reduce | flops 32 | bytes 256
  30.5 0.1 copy.32
  30.6 0.1 reduce-window.4
  30.7 0.8 fusion.82
  31.4 1.0 gather_fusion
  32.4 0.5 constant_dynamic-slice_fusion
  33.0 0.6 compare_and_fusion.2
  33.6 0.0 copy-done.3
  33.6 0.2 broadcast_select_fusion.3
  33.9 15.0 %gather_fusion.2 = bf16[256,2,25,128]{3,1,2,0:T(2,128)(2,1)} fusion(bf16[2,25,16,128]{3,0,2,1:T(2,128)(2,1)S(1)} %broadcast_select_fusion.3, s32[1024]{0:T(1024)S(1)} %pad_clamp_fusion.1), kind=kCustom, calls=%fused_computation.1.clone | custom fusion | bytes 6554624 | tf_op jit(solution)/shard_map/while/body/eval_jaxpr/jit(_take)/gather | solution.py:64
  48.9 2.3 gather_fusion.1
  51.2 6.8 fusion.16
  58.0 653.9 %all-gather.2.cloned.1.call-done = bf16[256,128,128]{2,1,0:T(8,128)(2,1)} async-done(((bf16[1,128,128]{2,1,0:T(8,128)(2,1)}), bf16[256,128,128]{2,1,0:T(8,128)(2,1)}) %all-gather.2.cloned.1.call-update) | async-done | bytes 8388624 | tf_op jit(solution)/shard_map/all_gather | solution.py:35
  711.9 0.0 copy-start.4
  711.9 8.1 fusion.12
  720.0 0.1 reshape.136
  720.1 0.1 reduce_sum.25
  720.2 45.2 %psum.7 = f32[1,64]{1,0:T(1,128)S(1)} all-reduce(f32[1,64]{1,0:T(1,128)S(1)} %bitcast.126), channel_id=1, replica_groups=mesh['walker'=32,'vec'=8] {'vec'}, use_global_device_ids=true, to_apply=%region_3.5 | all-reduce | flops 64 | bytes 512 | tf_op jit(solution)/shard_map/psum | solution.py:43
  765.4 0.0 collective-permute-done
  765.4 0.0 copy-done.4
  765.4 0.1 fusion.79
  765.5 0.1 broadcast_in_dim.63
  765.6 0.1 mul.35
  765.7 10.2 %fusion.19 = f32[2,25,256,128]{3,1,0,2:T(8,128)S(1)} fusion(bf16[256,128,128]{2,1,0:T(8,128)(2,1)} %all-gather.2.cloned.1.call-done, bf16[2,25,256,128]{3,0,1,2:T(2,128)(2,1)} %fusion.16), kind=kOutput, calls=%fused_computation.28 | convolution fusion | flops 419430400 | bytes 18219008 | tf_op jit(solution)/shard_map/while/body/eval_jaxpr/qitl,tkl->qitk/dot_general | solution.py:65
  775.9 6.8 fusion.58
  782.7 0.2 copy.38
  782.8 15.4 %gather_fusion.3 = bf16[256,2,25,128]{3,1,2,0:T(2,128)(2,1)} fusion(bf16[2,25,16,128]{3,0,2,1:T(2,128)(2,1)S(1)} %copy.38, s32[1024]{0:T(1024)S(1)} %pad_clamp_fusion.1), kind=kCustom, calls=%fused_computation.3.clone | custom fusion | bytes 6554624 | tf_op jit(solution)/shard_map/while/body/eval_jaxpr/jit(_take)/gather | solution.py:64
  798.2 5.0 fusion.17
  803.3 8.3 fusion.24
  811.6 6.8 fusion.61
  818.3 0.2 copy.42
  818.5 0.8 copy.41
  819.3 0.8 copy.37
  820.1 15.2 %gather_fusion.4 = bf16[256,2,25,128]{3,1,2,0:T(2,128)(2,1)} fusion(bf16[2,25,16,128]{3,0,2,1:T(2,128)(2,1)S(1)} %copy.42, s32[1024]{0:T(1024)S(1)} %pad_clamp_fusion.1), kind=kCustom, calls=%fused_computation.4.clone | custom fusion | bytes 6554624 | tf_op jit(solution)/shard_map/while/body/eval_jaxpr/jit(_take)/gather | solution.py:64
  835.2 5.0 fusion.18
  840.3 8.4 fusion.29
  848.7 0.0 copy-start.1
  848.7 0.0 copy-start.2
  848.7 6.8 fusion.49
  855.5 0.2 reshape.141
  855.7 0.0 copy-done.1
  855.7 0.2 reshape.140
  855.9 0.0 copy-done.2
  856.0 0.2 reshape.139
  856.2 0.6 add_convert_fusion
  856.7 0.2 slice.29
  857.0 1.9 collective-permute-start.1
  859.5 5.4 collective-permute-done.1
  864.9 0.3 broadcast_select_fusion.4
  865.2 0.7 copy.46
  (14 shorter events, 0.2 us)
Async XLA Ops:
  6.5 3.1 copy-start
  6.5 27.1 %copy-start.3 = (bf16[1,25,2048]{2,1,0:T(8,128)(2,1)S(1)}, bf16[1,25,2048]{2,1,0:T(8,128)(2,1)}, u32[]{:S(2)}) copy-start(bf16[1,25,2048]{2,1,0:T(8,128)(2,1)} %param.12) | copy-start | bytes 307204
  6.5 705.3 %all-gather.2.cloned.1.call-start = ((), (), s32[]{:S(2)}) async-start(), calls=%async_computation | async-start | bytes 8421376 | tf_op jit(solution)/shard_map/all_gather | solution.py:35
  7.3 758.2 %collective-permute-start = (f32[1,64]{1,0:T(1,128)}, f32[1,64]{1,0:T(1,128)S(1)}, u32[]{:S(2)}, u32[]{:S(2)}) collective-permute-start(f32[1,64]{1,0:T(1,128)} %param.17), channel_id=1, source_target_pairs={{8,0},{16,8},{24,16},{32,24},{40,32},{48,40},{56,48},{64,56},{72,6... | collective-permute-start | bytes 776 | tf_op jit(solution)/shard_map/ppermute | solution.py:15
  711.9 53.6 %copy-start.4 = (f32[1,64]{1,0:T(1,128)S(1)}, f32[1,64]{1,0:T(1,128)}, u32[]{:S(2)}) copy-start(f32[1,64]{1,0:T(1,128)} %param.17) | copy-start | bytes 772
  848.7 7.0 copy-start.1
  848.7 7.3 copy-start.2
  857.0 8.0 collective-permute-start.1
Sparse Core Ops, SparseCore 0:
  9.2 702.6 all-gather.1
where the time goes:
time: 882 us; the launch traced here: 873 us
  waiting for transfers between devices  660 us (75%)
  blocking collectives  61.4 us (7%)
  local copies, waits for them, and re-layouts  57 us (6%)
  matrix products  56.3 us (6%)
  other arithmetic  18.9 us (2%)
  between operations  15.4 us (2%)
    all_gather x1, waiting for transfers between devices, force_bias(): lax.all_gather(chol_tiles, ('walker', 'vec'), axis=0, tiled=True)  654 us
    gather x3, local copies, waits for them, and re-layouts, add_block(): chosen = jnp.take(series_blocks, col_blocks, axis=2)  45.5 us
    psum x1, blocking collectives, force_bias(): summed_bias = lax.psum(per_vector, 'vec')  45.2 us
    dot_general x3, matrix products, add_block(): jnp.einsum('qitl,tkl->qitk', chosen, stored, preferred_element_type=jnp.f...  26.9 us
    dot_general x3, matrix products, add_block(): jnp.einsum('qitk,qat->qiak', product, weights, precision=lax.Precision.HI...  20.3 us
  transfers between devices with their start and end apart: 3, of which 2 were waited for; matrix products, arithmetic and copies ran while one was open for 5% of the time, Pallas kernels for 0%

commit v1 on v0

--- a/solution.py
+++ b/solution.py
@@ -32,7 +32,12 @@
     ).astype(jnp.bfloat16)
     panel_blocks = walker_panels.reshape(walkers, cols_local, block_count, tile_size)
     green_blocks = green_rows.reshape(walkers, cols_local, block_count, tile_size)
-    tile_piece = lax.all_gather(chol_tiles, ("walker", "vec"), axis=0, tiled=True)
+    tile_piece = jnp.concatenate(
+        lax.all_to_all(
+            jnp.stack([chol_tiles] * lax.axis_size(("walker", "vec"))), ("walker", "vec"), 0, 0
+        ),
+        axis=0,
+    )
     contrib = tile_bias(
         tile_piece, tile_blocks[:, 0], tile_blocks[:, 1], panel_blocks, green_blocks
     )

time: 882 us -> 382 us (0.43)
  the two profiles are of different devices: /device:TPU:104 before, /device:TPU:32 now
where the time goes in v1:
time: 382 us; the launch traced here: 379 us
  blocking collectives  208 us (54%)
  matrix products  64.5 us (17%)
  local copies, waits for them, and re-layouts  59.9 us (16%)
  starting transfers between devices  20.3 us (5%)
  other arithmetic  18.8 us (5%)
  waiting for transfers between devices  5.36 us (1%)
    unnamed x1, blocking collectives  183 us
    gather x3, local copies, waits for them, and re-layouts, add_block(): chosen = jnp.take(series_blocks, col_blocks, axis=2)  45.3 us
    dot_general x3, matrix products, add_block(): jnp.einsum('qitl,tkl->qitk', chosen, stored, preferred_element_type=jnp.f...  27.1 us
    psum x1, blocking collectives, force_bias(): summed_bias = lax.psum(per_vector, 'vec')  24.9 us
    dot_general x3, matrix products, add_block(): jnp.einsum('qitk,qat->qiak', product, weights, precision=lax.Precision.HI...  20.3 us
    dot_general x1, matrix products, tile_bias(): jnp.einsum('wirl,rkl->wirk', chosen, tile_piece, preferred_element_type=j...  16.9 us
    select_n x3, other arithmetic, add_block(): chosen = jnp.take(series_blocks, col_blocks, axis=2)  16.8 us
    all_to_all x1, starting transfers between devices, force_bias(): lax.all_to_all(jnp.stack([chol_tiles] * lax.axis_size(('walker', 'vec')))...  15.4 us
  transfers between devices with their start and end apart: 3, of which 1 were waited for; matrix products, arithmetic and copies ran while one was open for 12% of the time, Pallas kernels for 0%

profile of v1, /device:TPU:32, one launch (start us, length us, event | category | flops | bytes accessed | tf_op | source)
XLA Modules:
  0.0 379.1 jit_solution(12549227429919406584)
XLA Ops:
  0.0 0.0 copy-start
  0.0 6.2 %stack.2 = bf16[256,1,128,128]{3,2,1,0:T(8,128)(2,1)} broadcast(bf16[128,128]{1,0:T(8,128)(2,1)} %bitcast.126), dimensions={2,3} | broadcast | bytes 8421376 | tf_op jit(solution)/shard_map/stack | solution.py:37
  6.2 0.0 copy-start.6
  6.2 0.0 copy-start.4
  6.2 0.0 copy-start.3
  6.2 0.0 copy-start.7
  6.2 0.0 copy-start.5
  6.2 15.4 %all-to-all-start = ((bf16[256,1,128,128]{3,2,1,0:T(8,128)(2,1)}), bf16[256,1,128,128]{3,2,1,0:T(8,128)(2,1)}, u32[]{:S(2)}, u32[]{:S(2)}) async-start(bf16[256,1,128,128]{3,2,1,0:T(8,128)(2,1)} %stack.2), calls=%async_computation | async-start | bytes 16777216 | tf_op jit(solution)/shard_map/all_to_all | solution.py:36
  21.6 0.0 copy-done.6
  21.6 3.0 collective-permute-start
  24.6 0.0 copy-done
  24.6 0.0 copy-done.4
  24.6 0.3 convolution_convert_fusion
  25.0 0.0 copy-done.3
  25.7 0.0 copy-done.7
  25.7 0.6 dynamic-slice.1
  26.3 0.7 dynamic-update-slice
  27.0 183.5 %all-reduce = s32[32]{0:T(128)S(1)} all-reduce(s32[32]{0:T(128)S(1)} %dynamic-update-slice), channel_id=1, replica_groups=mesh['walker'=32,'vec'=8] {'walker'}, use_global_device_ids=true, to_apply=%add | all-reduce | flops 32 | bytes 256
  210.4 0.1 copy.32
  210.5 0.1 reduce-window.4
  210.6 0.0 copy-done.5
  210.6 1.0 gather_fusion
  211.6 0.6 constant_dynamic-slice_fusion
  212.2 0.7 compare_and_fusion.2
  212.9 0.2 broadcast_select_fusion.3
  213.2 15.0 %gather_fusion.2 = bf16[256,2,25,128]{3,1,2,0:T(2,128)(2,1)} fusion(bf16[2,25,16,128]{3,0,2,1:T(2,128)(2,1)S(1)} %broadcast_select_fusion.3, s32[1024]{0:T(1024)S(1)} %pad_clamp_fusion.1), kind=kCustom, calls=%fused_computation.1.clone | custom fusion | bytes 6554624 | tf_op jit(solution)/shard_map/while/body/eval_jaxpr/jit(_take)/gather | solution.py:69
  228.2 2.2 gather_fusion.1
  230.4 6.7 %fusion.18 = bf16[2,25,256,128]{3,0,1,2:T(2,128)(2,1)} fusion(bf16[256,2,25,128]{3,1,2,0:T(2,128)(2,1)} %gather_fusion.2, pred[256]{0:T(512)(128)(4,1)S(1)} %get-tuple-element.50), kind=kLoop, calls=%fused_computation.27 | loop fusion | flops 1638400 | bytes 6553856 | tf_op jit(solution)/shard_map/while/body/eval_jaxpr/jit(_take)/select_n | solution.py:69
  237.1 0.0 all-to-all-done
  237.1 16.9 %fusion.14 = f32[256]{0:T(256)S(1)} fusion(bf16[256,1,128,128]{3,2,1,0:T(8,128)(2,1)} %all-to-all-done, bf16[256,25,128]{2,1,0:T(8,128)(2,1)} %gather_fusion.1, bf16[256,25,128]{2,1,0:T(8,128)(2,1)S(1)} %gather_fusion, pred[256]{0:T(512)(128)(4,1)S(1)} %get-tuple-element.49, pred[256]{0:T(512)(128)(4,1)S(1)} %get-tuple-element.50), kind=kOutput, calls=%fused_computation.23 | convolution fusion | flops 213810944 | bytes 11666944 | tf_op jit(solution)/shard_map/wirl,rkl->wirk/dot_general | solution.py:20
  254.0 0.1 reshape.143
  254.1 0.1 reduce_sum.25
  254.2 24.9 %psum.7 = f32[1,64]{1,0:T(1,128)S(1)} all-reduce(f32[1,64]{1,0:T(1,128)S(1)} %bitcast.132), channel_id=1, replica_groups=mesh['walker'=32,'vec'=8] {'vec'}, use_global_device_ids=true, to_apply=%region_3.5 | all-reduce | flops 64 | bytes 512 | tf_op jit(solution)/shard_map/psum | solution.py:48
  279.1 0.0 collective-permute-done
  279.1 0.1 fusion.83
  279.2 0.1 broadcast_in_dim.63
  279.3 0.1 mul.35
  279.4 10.2 %fusion.21 = f32[2,25,256,128]{3,1,0,2:T(8,128)S(1)} fusion(bf16[256,1,128,128]{3,2,1,0:T(8,128)(2,1)} %all-to-all-done, bf16[2,25,256,128]{3,0,1,2:T(2,128)(2,1)} %fusion.18), kind=kOutput, calls=%fused_computation.30 | convolution fusion | flops 419430400 | bytes 18219008 | tf_op jit(solution)/shard_map/while/body/eval_jaxpr/qitl,tkl->qitk/dot_general | solution.py:70
  289.6 6.8 %fusion.62 = bf16[2,25,16,128]{3,2,1,0:T(8,128)(2,1)S(1)} fusion(f32[2,25,256,128]{3,1,0,2:T(8,128)S(1)} %fusion.21, f32[16,256]{1,0:T(8,128)S(1)} %fusion.82, f32[2,256]{1,0:T(2,128)S(1)} %mul.35), kind=kOutput, calls=%fused_computation.45 | convolution fusion | flops 314683392 | bytes 6776832 | tf_op jit(solution)/shard_map/while/body/eval_jaxpr/qitk,qat->qiak/dot_general | solution.py:73
  296.4 0.2 copy.38
  296.5 15.2 %gather_fusion.3 = bf16[256,2,25,128]{3,1,2,0:T(2,128)(2,1)} fusion(bf16[2,25,16,128]{3,0,2,1:T(2,128)(2,1)S(1)} %copy.38, s32[1024]{0:T(1024)S(1)} %pad_clamp_fusion.1), kind=kCustom, calls=%fused_computation.3.clone | custom fusion | bytes 6554624 | tf_op jit(solution)/shard_map/while/body/eval_jaxpr/jit(_take)/gather | solution.py:69
  311.7 5.0 %fusion.19 = bf16[2,25,256,128]{3,0,1,2:T(2,128)(2,1)S(1)} fusion(bf16[256,2,25,128]{3,1,2,0:T(2,128)(2,1)} %gather_fusion.3, pred[256]{0:T(512)(128)(4,1)S(1)} %get-tuple-element.50), kind=kLoop, calls=%fused_computation.28 | loop fusion | flops 1638400 | bytes 6553856 | tf_op jit(solution)/shard_map/while/body/eval_jaxpr/jit(_take)/select_n | solution.py:69
  316.8 8.5 %fusion.26 = f32[2,25,256,128]{3,1,0,2:T(8,128)S(1)} fusion(bf16[256,1,128,128]{3,2,1,0:T(8,128)(2,1)} %all-to-all-done, bf16[2,25,256,128]{3,0,1,2:T(2,128)(2,1)S(1)} %fusion.19), kind=kOutput, calls=%fused_computation.31 | convolution fusion | flops 419430400 | bytes 18219008 | tf_op jit(solution)/shard_map/while/body/eval_jaxpr/qitl,tkl->qitk/dot_general | solution.py:70
  325.3 6.8 %fusion.65 = bf16[2,25,16,128]{3,2,1,0:T(8,128)(2,1)S(1)} fusion(f32[2,25,256,128]{3,1,0,2:T(8,128)S(1)} %fusion.26, f32[16,256]{1,0:T(8,128)S(1)} %fusion.82, f32[2,256]{1,0:T(2,128)S(1)} %mul.35), kind=kOutput, calls=%fused_computation.46 | convolution fusion | flops 314785792 | bytes 6776832 | tf_op jit(solution)/shard_map/while/body/eval_jaxpr/qitk,qat->qiak/dot_general | solution.py:73
  332.1 0.2 copy.42
  332.3 0.8 copy.37
  333.1 15.1 %gather_fusion.4 = bf16[256,2,25,128]{3,1,2,0:T(2,128)(2,1)} fusion(bf16[2,25,16,128]{3,0,2,1:T(2,128)(2,1)S(1)} %copy.42, s32[1024]{0:T(1024)S(1)} %pad_clamp_fusion.1), kind=kCustom, calls=%fused_computation.4.clone | custom fusion | bytes 6554624 | tf_op jit(solution)/shard_map/while/body/eval_jaxpr/jit(_take)/gather | solution.py:69
  348.2 5.0 %fusion.20 = bf16[2,25,256,128]{3,0,1,2:T(2,128)(2,1)S(1)} fusion(bf16[256,2,25,128]{3,1,2,0:T(2,128)(2,1)} %gather_fusion.4, pred[256]{0:T(512)(128)(4,1)S(1)} %get-tuple-element.50), kind=kLoop, calls=%fused_computation.29 | loop fusion | flops 1638400 | bytes 6553856 | tf_op jit(solution)/shard_map/while/body/eval_jaxpr/jit(_take)/select_n | solution.py:69
  353.2 8.3 %fusion.31 = f32[2,25,256,128]{3,1,0,2:T(8,128)S(1)} fusion(bf16[256,1,128,128]{3,2,1,0:T(8,128)(2,1)} %all-to-all-done, bf16[2,25,256,128]{3,0,1,2:T(2,128)(2,1)S(1)} %fusion.20), kind=kOutput, calls=%fused_computation.32 | convolution fusion | flops 419430400 | bytes 18219008 | tf_op jit(solution)/shard_map/while/body/eval_jaxpr/qitl,tkl->qitk/dot_general | solution.py:70
  361.6 0.0 copy-start.2
  361.6 0.0 copy-start.1
  361.6 6.8 %fusion.53 = f32[2,25,16,128]{3,2,1,0:T(8,128)S(1)} fusion(f32[2,25,256,128]{3,1,0,2:T(8,128)S(1)} %fusion.31, f32[16,256]{1,0:T(8,128)S(1)} %fusion.82, f32[2,256]{1,0:T(2,128)S(1)} %mul.35), kind=kOutput, calls=%fused_computation.42 | convolution fusion | flops 314888192 | bytes 6981632 | tf_op jit(solution)/shard_map/while/body/eval_jaxpr/qitk,qat->qiak/dot_general | solution.py:73
  368.4 0.2 reshape.148
  368.6 0.2 reshape.147
  368.9 0.0 copy-done.2
  368.9 0.2 reshape.146
  369.1 0.5 add_convert_fusion
  369.6 0.2 slice.29
  369.9 1.9 collective-permute-start.1
  372.5 5.4 %collective-permute-done.1 = bf16[1,25,2048]{2,0,1:T(2,128)(2,1)S(1)} collective-permute-done((bf16[1,25,2048]{2,0,1:T(2,128)(2,1)S(1)}, bf16[1,25,2048]{2,0,1:T(2,128)(2,1)S(1)}, u32[]{:S(2)}, u32[]{:S(2)}) %collective-permute-start.1) | collective-permute-done | bytes 102432 | tf_op jit(solution)/shard_map/ppermute | solution.py:15
  377.8 0.3 broadcast_select_fusion.4
  378.1 0.7 copy.46
  378.8 0.0 copy-done.1
  (17 shorter events, 0.3 us)
Async XLA Ops:
  0.0 24.6 %copy-start = (bf16[200,2048]{1,0:T(8,128)(2,1)S(1)}, bf16[200,2048]{1,0:T(8,128)(2,1)}, u32[]{:S(2)}) copy-start(bf16[200,2048]{1,0:T(8,128)(2,1)} %param.14) | copy-start | bytes 2457604
  6.2 15.4 %copy-start.6 = (f32[1,64]{1,0:T(1,128)S(1)}, f32[1,64]{1,0:T(1,128)}, u32[]{:S(2)}) copy-start(f32[1,64]{1,0:T(1,128)} %param.17) | copy-start | bytes 772
  6.2 18.4 %copy-start.4 = (bf16[1,25,200]{2,1,0:T(8,128)(2,1)S(1)}, bf16[1,25,200]{2,1,0:T(8,128)(2,1)}, u32[]{:S(2)}) copy-start(bf16[1,25,200]{2,1,0:T(8,128)(2,1)} %param.13) | copy-start | bytes 30004
  6.2 18.8 %copy-start.3 = (bf16[1,25,2048]{2,1,0:T(8,128)(2,1)S(1)}, bf16[1,25,2048]{2,1,0:T(8,128)(2,1)}, u32[]{:S(2)}) copy-start(bf16[1,25,2048]{2,1,0:T(8,128)(2,1)} %param.12) | copy-start | bytes 307204
  6.2 19.5 %copy-start.7 = (u32[256]{0:T(256)S(1)}, u32[256]{0:T(256)}, u32[]{:S(2)}) copy-start(u32[256]{0:T(256)} %constant.93) | copy-start | bytes 3076
  6.2 204.4 %copy-start.5 = (s32[256,2]{0,1:T(2,128)S(1)}, s32[256,2]{0,1:T(2,128)}, u32[]{:S(2)}) copy-start(s32[256,2]{0,1:T(2,128)} %param.16) | copy-start | bytes 6148
  6.2 230.9 %all-to-all-start = ((bf16[256,1,128,128]{3,2,1,0:T(8,128)(2,1)}), bf16[256,1,128,128]{3,2,1,0:T(8,128)(2,1)}, u32[]{:S(2)}, u32[]{:S(2)}) async-start(bf16[256,1,128,128]{3,2,1,0:T(8,128)(2,1)} %stack.2), calls=%async_computation | async-start | bytes 16777216 | tf_op jit(solution)/shard_map/all_to_all | solution.py:36
  21.6 257.5 %collective-permute-start = (f32[1,64]{1,0:T(1,128)S(1)}, f32[1,64]{1,0:T(1,128)S(1)}, u32[]{:S(2)}, u32[]{:S(2)}) collective-permute-start(f32[1,64]{1,0:T(1,128)S(1)} %copy-done.6), channel_id=1, source_target_pairs={{8,0},{16,8},{24,16},{32,24},{40,32},{48,40},{56,48},{64,56},{72,6... | collective-permute-start | bytes 776 | tf_op jit(solution)/shard_map/ppermute | solution.py:15
  361.6 7.3 %copy-start.2 = (f32[2,25,16,128]{3,2,0,1:T(8,128)S(1)}, f32[2,25,16,128]{3,2,0,1:T(8,128)}, u32[]{:S(2)}) copy-start(f32[2,25,16,128]{3,2,0,1:T(8,128)} %copy.37) | copy-start | bytes 1228804
  361.6 17.3 %copy-start.1 = (bf16[200,2048]{1,0:T(8,128)(2,1)S(1)}, bf16[200,2048]{1,0:T(8,128)(2,1)}, u32[]{:S(2)}) copy-start(bf16[200,2048]{1,0:T(8,128)(2,1)} %param.14) | copy-start | bytes 2457604
  369.9 8.0 %collective-permute-start.1 = (bf16[1,25,2048]{2,0,1:T(2,128)(2,1)S(1)}, bf16[1,25,2048]{2,0,1:T(2,128)(2,1)S(1)}, u32[]{:S(2)}, u32[]{:S(2)}) collective-permute-start(bf16[1,25,2048]{2,0,1:T(2,128)(2,1)S(1)} %slice.29), channel_id=1, source_target_pairs={{0,8},{8,16},{16,24},{24,32},{32,40},{40,48},{48,56},{56,64},{64,7... | collective-permute-start | bytes 307208 | tf_op jit(solution)/shard_map/ppermute | solution.py:15
